TPU v7x, 32 devices: a whole 2x2x4 slice. The times are simulated.
32 devices in a mesh: tok: 8 (over z, core), head: 4 (over y, x).
Axes of the slice: x: 2, y: 2, z: 4, core: 2. Of those that a mesh axis runs over, the one named last changes fastest.
Arguments:
- query_states: bfloat16 [12288, 3072], P('tok', 'head')
- key_states: bfloat16 [12288, 3072], P('tok', 'head')
- value_states: bfloat16 [12288, 3072], P('tok', 'head'), may hold values from -6 to 6
- query_gain: float32 [3072], P('head'), may hold values from 1 to 2.5
- key_gain: float32 [3072], P('head'), may hold values from 1 to 2.5
- windows: int32 [48, 27], P('tok'), may hold values from -1 to 47, as said below
Outputs:
- attention: bfloat16 [12288, 3072], P('tok', 'head')
Inputs may be any that keep to these rules, and one draw needn't show every extreme that they name: Slots 0 to 8 of windows[i] name tiles of the tile-frame before tile i's, the next 9 tiles of its own tile-frame, the last 9 tiles of the tile-frame after it; in each group the named tiles come first and -1 fills the rest; tile i itself is always named; no tile is named twice in a row; a named tile's tile row and tile column differ from tile i's by at most 2 each, and some named tiles differ by 2 in both.
All inputs are finite; a program needn't handle non-finite values.
Results may differ from a plain program's by a relative error of at most 0.012.
The roundings to bfloat16 on the way count: a program that leaves them out, or rounds other values in their place, can miss the bound.
Values may be sent and summed in bfloat16 or wider, within the bound.
No kernel may reach another device: no remote copies, remote signals or barrier semaphores. Data moves between devices by JAX's collectives and lax.ppermute only.
A program may use at most 320 MiB of HBM per device.

v0:
```python
import math
import jax
import jax.numpy as jnp
from jax import lax
from jax.sharding import PartitionSpec as P

HEAD_DIM = 128
MODEL_DIM = 3072
TILE_TOKENS = 256
WINDOW_SLOTS = 27


def square_sums(source):
    widened = source.astype(jnp.float32)
    return jnp.sum(widened * widened, axis=1)


def normalize_rows(source, totals, scale_gain):
    widened = source.astype(jnp.float32)
    return (widened * lax.rsqrt(totals[:, None] / MODEL_DIM + 1e-06) * scale_gain).astype(
        jnp.bfloat16
    )


def on_device(query_states, key_states, value_states, query_gain, key_gain, windows):
    row_count = query_states.shape[0]
    local_width = query_states.shape[1]
    local_tiles = windows.shape[0]
    query_total, key_total = lax.psum((square_sums(query_states), square_sums(key_states)), "head")
    query_normed = normalize_rows(query_states, query_total, query_gain)
    sent_keys = normalize_rows(key_states, key_total, key_gain)
    paired = jnp.stack([sent_keys, value_states])
    extended = lax.all_gather(paired, "tok", axis=1, tiled=True)
    key_window_rows = extended[0]
    heads_here = local_width // HEAD_DIM
    key_tiles = key_window_rows.reshape(-1, TILE_TOKENS, local_width)
    value_tiles = extended[1].reshape(-1, TILE_TOKENS, local_width)
    query_tiles = query_normed.reshape(local_tiles, TILE_TOKENS, local_width)
    valid_slots = windows >= 0
    local_ids = jnp.where(valid_slots, windows, 0)
    block_count = local_tiles // 2
    score_scale = 1.0 / math.sqrt(HEAD_DIM)

    def attend(block_index):
        block_start = block_index * 2
        query_block = lax.dynamic_slice_in_dim(query_tiles, block_start, 2, 0)
        tile_ids = lax.dynamic_slice_in_dim(local_ids, block_start, 2, 0)
        live_slots = lax.dynamic_slice_in_dim(valid_slots, block_start, 2, 0)
        key_window = key_tiles[tile_ids].reshape(2, WINDOW_SLOTS * TILE_TOKENS, local_width)
        value_window = value_tiles[tile_ids].reshape(2, WINDOW_SLOTS * TILE_TOKENS, local_width)
        key_mask = jnp.repeat(live_slots, TILE_TOKENS, axis=1)[:, None, :]
        results = []
        for head_number in range(heads_here):
            lower = head_number * HEAD_DIM
            upper = lower + HEAD_DIM
            scores = (
                jnp.einsum(
                    "tqd,tkd->tqk",
                    query_block[:, :, lower:upper],
                    key_window[:, :, lower:upper],
                    preferred_element_type=jnp.float32,
                )
                * score_scale
            )
            scores = jnp.where(key_mask, scores, -jnp.inf)
            row_max = jnp.max(scores, axis=2, keepdims=True)
            weights = jnp.exp(scores - row_max)
            weight_sum = jnp.sum(weights, axis=2, keepdims=True)
            mixed = jnp.einsum(
                "tqk,tkd->tqd",
                weights.astype(jnp.bfloat16),
                value_window[:, :, lower:upper],
                preferred_element_type=jnp.float32,
            )
            results.append((mixed / weight_sum).astype(jnp.bfloat16))
        return jnp.concatenate(results, axis=2)

    outputs = lax.map(attend, jnp.arange(block_count, dtype=jnp.int32))
    return outputs.reshape(row_count, local_width)


def solution(mesh):
    in_specs = (
        P("tok", "head"),
        P("tok", "head"),
        P("tok", "head"),
        P("head"),
        P("head"),
        P("tok", None),
    )
    out_specs = P("tok", "head")
    return jax.shard_map(
        on_device, mesh=mesh, in_specs=in_specs, out_specs=out_specs, check_vma=False
    )
```

profile of v0, /device:TPU:0, one launch (start us, length us, event | category | flops | bytes accessed | tf_op | source)
XLA Modules:
  0.0 967.4 jit_solution(3506104877108742249)
XLA Ops:
  6.5 2.4 fusion.168
  8.9 2.2 fusion.171
  11.1 17.5 %all-reduce = (f32[1536]{0:T(1024)S(1)}, f32[1536]{0:T(1024)S(1)}) all-reduce(f32[1536]{0:T(1024)S(1)} %fusion.168, f32[1536]{0:T(1024)S(1)} %fusion.171), channel_id=1, replica_groups=mesh['tok'=8,'head'=4] {'head'}, use_global_device_ids=true, to_apply=%region_1.0 | all-reduce | flops 3072 | bytes 24576 | tf_op jit(solution)/shard_map/psum | solution.py:29
  28.6 2.3 fusion.174
  30.9 4.3 pad_maximum_fusion
  35.3 2.0 fusion.170
  37.3 320.6 %all-gather.2.cloned.1.call-done = bf16[2,12288,768]{2,1,0:T(8,128)(2,1)} async-done(((bf16[2,1536,768]{2,1,0:T(8,128)(2,1)}), bf16[2,12288,768]{2,1,0:T(8,128)(2,1)}) %all-gather.2.cloned.1.call-update) | async-done | bytes 37748752 | tf_op jit(solution)/shard_map/all_gather | solution.py:33
  357.9 26.5 %fusion.175 = (bf16[1,12288,768]{2,1,0:T(8,128)(2,1)}, bf16[1,12288,768]{2,1,0:T(8,128)(2,1)}) fusion(bf16[2,12288,768]{2,1,0:T(8,128)(2,1)} %all-gather.2.cloned.1.call-done), kind=kLoop, calls=%fused_computation.126 | loop fusion | bytes 75497472 | tf_op jit(solution)/shard_map/slice | solution.py:37
  384.4 575.9 %while.10 = (s32[]{:T(128)}, bf16[3,2,256,768]{3,2,1,0:T(8,128)(2,1)}, s32[3]{0:T(128)S(1)}, pred[6,27]{1,0:T(8,128)(4,1)S(1)}, bf16[6,256,768]{2,1,0:T(8,128)(2...) while((s32[]{:T(128)}, ...), condition=%wide.region_17.18_spmd, body=%wide.region_4.17_spmd.sunk | while | flops 11105987584 | bytes 443850720 | solution.py:78
  384.6 0.7 dynamic_slice.22
  386.0 0.1 reshape.71
  386.1 15.5 %gather_fusion.1 = bf16[54,256,768]{2,1,0:T(8,128)(2,1)} fusion(bf16[48,256,768]{2,1,0:T(8,128)(2,1)} %get-tuple-element.201, s32[1024]{0:T(1024)S(1)} %pad_clamp_fusion.2), kind=kCustom, calls=%fused_computation.clone.1 | custom fusion | bytes 42467544 | tf_op jit(solution)/shard_map/while/body/eval_jaxpr/gather | solution.py:49
  401.6 9.1 fusion.229
  410.8 10.7 %fusion.230 = (f32[2,256]{1,0:T(2,128)S(1)}, f32[2,256]{1,0:T(2,128)S(1)}, f32[2,256,6912]{2,1,0:T(8,128)}) fusion(pred[2,6912]{1,0:T(4,128)(4,1)S(1)} %bitcast.41, f32[2,256,6912]{2,1,0:T(8,128)} %fusion.229, bf16[2,6912,768]{2,1,0:T(8,128)(2,1)} %bitcast.27, bf16[6,256,768]{2,1,0:T(8,128)(2,1)} %get-tuple-element.199, s32[]{:T(128)S(6)} %select_n.152, ...), kind=kOutput, calls=%fused_computation.19.clone.1 | convolution fusion | flops 927202304 | bytes 31999496 | tf_op jit(solution)/shard_map/while/body/eval_jaxpr/tqd,tkd->tqk/dot_general | solution.py:57
  421.5 9.2 fusion.231
  430.7 9.0 fusion.232
  439.7 9.1 fusion.233
  448.9 31.3 %fusion.234 = (f32[2,256]{1,0:T(2,128)S(1)}, f32[2,256]{1,0:T(2,128)S(1)}, f32[2,256]{1,0:T(2,128)S(1)}, f32[2,256]{1,0:T(2,128)S(1)}, f32[2,256]{1,0:T(2,128)S(...) fusion(f32[2,256,6912]{2,1,0:T(8,128)} %get-tuple-element.148, f32[2,256]{1,0:T(2,128)S(1)} %get-tuple-element.149, ...), kind=kOutput, calls=%fused_computation.30.clone.1 | convolution fusion | flops 976745472 | bytes 88634888 | tf_op jit(solution)/shard_map/while/body/eval_jaxpr/tqd,tkd->tqk/dot_general | solution.py:57
  480.1 21.1 %fusion.236 = (f32[2,256]{1,0:T(2,128)S(1)}, f32[2,256]{1,0:T(2,128)S(1)}, f32[2,256]{1,0:T(2,128)S(1)}, f32[2,256]{1,0:T(2,128)S(1)}) fusion(f32[2,256,6912]{2,1,0:T(8,128)} %fusion.233, f32[2,256]{1,0:T(2,128)S(1)} %get-tuple-element.153, pred[2,6912]{1,0:T(4,128)(4,1)S(1)} %bitcast.43, f32[2,256]{1,0:T(2,128)S(1)} %get-tuple-element.152, ...), kind=kLoop, calls=%fused_computation.28.clone.1 | loop fusion | flops 56621056 | bytes 56653312 | tf_op jit(solution)/shard_map/while/body/eval_jaxpr/reduce_sum | solution.py:68
  501.2 16.1 %gather_fusion = bf16[54,256,768]{2,1,0:T(8,128)(2,1)} fusion(bf16[48,256,768]{2,1,0:T(8,128)(2,1)} %get-tuple-element.202, s32[1024]{0:T(1024)S(1)} %pad_clamp_fusion.2), kind=kCustom, calls=%fused_computation.1.clone.1 | custom fusion | bytes 42467544 | tf_op jit(solution)/shard_map/while/body/eval_jaxpr/gather | solution.py:50
  517.3 9.5 fusion.235
  526.8 9.5 fusion.237
  536.4 9.6 fusion.238
  545.9 9.7 %fusion.239 = bf16[2,256,768]{1,2,0:T(8,128)(2,1)S(1)} fusion(bf16[2,256,768]{1,2,0:T(8,128)(2,1)S(1)} %fusion.238, bf16[2,6912,768]{2,1,0:T(8,128)(2,1)} %bitcast.37, f32[2,256,6912]{2,1,0:T(8,128)} %fusion.232, f32[2,256]{1,0:T(2,128)S(1)} %get-tuple-element.155, pred[2,6912]{1,0:T(4,128)(4,1)S(1)} %bitcast.47, f32[2,256]{1,0:T(2,128)S(1)} %get-tuple-element.158), kind=kOutput, calls=%fused_computation.73.clone.1 | convolution fusion | flops 920256512 | bytes 17857536 | tf_op jit(solution)/shard_map/while/body/eval_jaxpr/tqk,tkd->tqd/dot_general | solution.py:69
  555.7 9.6 fusion.240
  565.2 9.6 fusion.241
  574.8 0.3 copy.27
  575.1 0.9 constant_dynamic-update-slice_fusion.2
  576.2 0.7 dynamic_slice.22
  577.7 15.6 %gather_fusion.1 = bf16[54,256,768]{2,1,0:T(8,128)(2,1)} fusion(bf16[48,256,768]{2,1,0:T(8,128)(2,1)} %get-tuple-element.201, s32[1024]{0:T(1024)S(1)} %pad_clamp_fusion.2), kind=kCustom, calls=%fused_computation.clone.1 | custom fusion | bytes 42467544 | tf_op jit(solution)/shard_map/while/body/eval_jaxpr/gather | solution.py:49
  593.3 9.1 fusion.229
  602.5 10.7 %fusion.230 = (f32[2,256]{1,0:T(2,128)S(1)}, f32[2,256]{1,0:T(2,128)S(1)}, f32[2,256,6912]{2,1,0:T(8,128)}) fusion(pred[2,6912]{1,0:T(4,128)(4,1)S(1)} %bitcast.41, f32[2,256,6912]{2,1,0:T(8,128)} %fusion.229, bf16[2,6912,768]{2,1,0:T(8,128)(2,1)} %bitcast.27, bf16[6,256,768]{2,1,0:T(8,128)(2,1)} %get-tuple-element.199, s32[]{:T(128)S(6)} %select_n.152, ...), kind=kOutput, calls=%fused_computation.19.clone.1 | convolution fusion | flops 927202304 | bytes 31999496 | tf_op jit(solution)/shard_map/while/body/eval_jaxpr/tqd,tkd->tqk/dot_general | solution.py:57
  613.2 9.2 fusion.231
  622.4 9.0 fusion.232
  631.4 9.1 fusion.233
  640.6 31.3 %fusion.234 = (f32[2,256]{1,0:T(2,128)S(1)}, f32[2,256]{1,0:T(2,128)S(1)}, f32[2,256]{1,0:T(2,128)S(1)}, f32[2,256]{1,0:T(2,128)S(1)}, f32[2,256]{1,0:T(2,128)S(...) fusion(f32[2,256,6912]{2,1,0:T(8,128)} %get-tuple-element.148, f32[2,256]{1,0:T(2,128)S(1)} %get-tuple-element.149, ...), kind=kOutput, calls=%fused_computation.30.clone.1 | convolution fusion | flops 976745472 | bytes 88634888 | tf_op jit(solution)/shard_map/while/body/eval_jaxpr/tqd,tkd->tqk/dot_general | solution.py:57
  671.9 21.1 %fusion.236 = (f32[2,256]{1,0:T(2,128)S(1)}, f32[2,256]{1,0:T(2,128)S(1)}, f32[2,256]{1,0:T(2,128)S(1)}, f32[2,256]{1,0:T(2,128)S(1)}) fusion(f32[2,256,6912]{2,1,0:T(8,128)} %fusion.233, f32[2,256]{1,0:T(2,128)S(1)} %get-tuple-element.153, pred[2,6912]{1,0:T(4,128)(4,1)S(1)} %bitcast.43, f32[2,256]{1,0:T(2,128)S(1)} %get-tuple-element.152, ...), kind=kLoop, calls=%fused_computation.28.clone.1 | loop fusion | flops 56621056 | bytes 56653312 | tf_op jit(solution)/shard_map/while/body/eval_jaxpr/reduce_sum | solution.py:68
  693.0 15.8 %gather_fusion = bf16[54,256,768]{2,1,0:T(8,128)(2,1)} fusion(bf16[48,256,768]{2,1,0:T(8,128)(2,1)} %get-tuple-element.202, s32[1024]{0:T(1024)S(1)} %pad_clamp_fusion.2), kind=kCustom, calls=%fused_computation.1.clone.1 | custom fusion | bytes 42467544 | tf_op jit(solution)/shard_map/while/body/eval_jaxpr/gather | solution.py:50
  708.8 9.6 fusion.235
  718.3 9.6 fusion.237
  727.9 9.6 fusion.238
  737.4 9.8 %fusion.239 = bf16[2,256,768]{1,2,0:T(8,128)(2,1)S(1)} fusion(bf16[2,256,768]{1,2,0:T(8,128)(2,1)S(1)} %fusion.238, bf16[2,6912,768]{2,1,0:T(8,128)(2,1)} %bitcast.37, f32[2,256,6912]{2,1,0:T(8,128)} %fusion.232, f32[2,256]{1,0:T(2,128)S(1)} %get-tuple-element.155, pred[2,6912]{1,0:T(4,128)(4,1)S(1)} %bitcast.47, f32[2,256]{1,0:T(2,128)S(1)} %get-tuple-element.158), kind=kOutput, calls=%fused_computation.73.clone.1 | convolution fusion | flops 920256512 | bytes 17857536 | tf_op jit(solution)/shard_map/while/body/eval_jaxpr/tqk,tkd->tqd/dot_general | solution.py:69
  747.2 9.6 fusion.240
  756.8 9.6 fusion.241
  766.3 0.3 copy.27
  766.6 0.9 constant_dynamic-update-slice_fusion.2
  767.9 0.7 dynamic_slice.22
  769.4 15.6 %gather_fusion.1 = bf16[54,256,768]{2,1,0:T(8,128)(2,1)} fusion(bf16[48,256,768]{2,1,0:T(8,128)(2,1)} %get-tuple-element.201, s32[1024]{0:T(1024)S(1)} %pad_clamp_fusion.2), kind=kCustom, calls=%fused_computation.clone.1 | custom fusion | bytes 42467544 | tf_op jit(solution)/shard_map/while/body/eval_jaxpr/gather | solution.py:49
  785.0 9.0 fusion.229
  794.2 10.7 %fusion.230 = (f32[2,256]{1,0:T(2,128)S(1)}, f32[2,256]{1,0:T(2,128)S(1)}, f32[2,256,6912]{2,1,0:T(8,128)}) fusion(pred[2,6912]{1,0:T(4,128)(4,1)S(1)} %bitcast.41, f32[2,256,6912]{2,1,0:T(8,128)} %fusion.229, bf16[2,6912,768]{2,1,0:T(8,128)(2,1)} %bitcast.27, bf16[6,256,768]{2,1,0:T(8,128)(2,1)} %get-tuple-element.199, s32[]{:T(128)S(6)} %select_n.152, ...), kind=kOutput, calls=%fused_computation.19.clone.1 | convolution fusion | flops 927202304 | bytes 31999496 | tf_op jit(solution)/shard_map/while/body/eval_jaxpr/tqd,tkd->tqk/dot_general | solution.py:57
  804.9 9.2 fusion.231
  814.1 9.0 fusion.232
  823.2 9.1 fusion.233
  832.3 31.1 %fusion.234 = (f32[2,256]{1,0:T(2,128)S(1)}, f32[2,256]{1,0:T(2,128)S(1)}, f32[2,256]{1,0:T(2,128)S(1)}, f32[2,256]{1,0:T(2,128)S(1)}, f32[2,256]{1,0:T(2,128)S(...) fusion(f32[2,256,6912]{2,1,0:T(8,128)} %get-tuple-element.148, f32[2,256]{1,0:T(2,128)S(1)} %get-tuple-element.149, ...), kind=kOutput, calls=%fused_computation.30.clone.1 | convolution fusion | flops 976745472 | bytes 88634888 | tf_op jit(solution)/shard_map/while/body/eval_jaxpr/tqd,tkd->tqk/dot_general | solution.py:57
  863.4 21.1 %fusion.236 = (f32[2,256]{1,0:T(2,128)S(1)}, f32[2,256]{1,0:T(2,128)S(1)}, f32[2,256]{1,0:T(2,128)S(1)}, f32[2,256]{1,0:T(2,128)S(1)}) fusion(f32[2,256,6912]{2,1,0:T(8,128)} %fusion.233, f32[2,256]{1,0:T(2,128)S(1)} %get-tuple-element.153, pred[2,6912]{1,0:T(4,128)(4,1)S(1)} %bitcast.43, f32[2,256]{1,0:T(2,128)S(1)} %get-tuple-element.152, ...), kind=kLoop, calls=%fused_computation.28.clone.1 | loop fusion | flops 56621056 | bytes 56653312 | tf_op jit(solution)/shard_map/while/body/eval_jaxpr/reduce_sum | solution.py:68
  884.5 15.8 %gather_fusion = bf16[54,256,768]{2,1,0:T(8,128)(2,1)} fusion(bf16[48,256,768]{2,1,0:T(8,128)(2,1)} %get-tuple-element.202, s32[1024]{0:T(1024)S(1)} %pad_clamp_fusion.2), kind=kCustom, calls=%fused_computation.1.clone.1 | custom fusion | bytes 42467544 | tf_op jit(solution)/shard_map/while/body/eval_jaxpr/gather | solution.py:50
  900.3 9.5 fusion.235
  909.9 9.5 fusion.237
  919.4 9.6 fusion.238
  929.0 9.9 %fusion.239 = bf16[2,256,768]{1,2,0:T(8,128)(2,1)S(1)} fusion(bf16[2,256,768]{1,2,0:T(8,128)(2,1)S(1)} %fusion.238, bf16[2,6912,768]{2,1,0:T(8,128)(2,1)} %bitcast.37, f32[2,256,6912]{2,1,0:T(8,128)} %fusion.232, f32[2,256]{1,0:T(2,128)S(1)} %get-tuple-element.155, pred[2,6912]{1,0:T(4,128)(4,1)S(1)} %bitcast.47, f32[2,256]{1,0:T(2,128)S(1)} %get-tuple-element.158), kind=kOutput, calls=%fused_computation.73.clone.1 | convolution fusion | flops 920256512 | bytes 17857536 | tf_op jit(solution)/shard_map/while/body/eval_jaxpr/tqk,tkd->tqd/dot_general | solution.py:69
  938.9 9.6 fusion.240
  948.5 9.6 fusion.241
  958.1 0.3 copy.27
  958.3 0.9 constant_dynamic-update-slice_fusion.2
  (30 shorter events, 0.6 us)
Async XLA Ops:
  6.5 28.7 %copy-start = (bf16[1536,768]{1,0:T(8,128)(2,1)S(1)}, bf16[1536,768]{1,0:T(8,128)(2,1)}, u32[]{:S(2)}) copy-start(bf16[1536,768]{1,0:T(8,128)(2,1)} %param.8) | copy-start | bytes 7077892
  6.5 28.7 %copy-start.1 = (s32[6,27]{1,0:T(8,128)S(1)}, s32[6,27]{1,0:T(8,128)}, u32[]{:S(2)}) copy-start(s32[6,27]{1,0:T(8,128)} %param.13) | copy-start | bytes 1948
  6.5 28.7 %copy-start.2 = (f32[768]{0:T(1024)S(1)}, f32[768]{0:T(1024)}, u32[]{:S(2)}) copy-start(f32[768]{0:T(1024)} %param.11) | copy-start | bytes 9220
  6.5 351.4 %all-gather.2.cloned.1.call-start = ((), (), s32[]{:S(2)}) async-start(), calls=%async_computation | async-start | bytes 42467328 | tf_op jit(solution)/shard_map/all_gather | solution.py:33
Sparse Core Ops, SparseCore 0:
  35.3 322.5 all-gather.1
where the time goes:
time: 971 us; the launch traced here: 967 us
  matrix products  408 us (42%)
  waiting for transfers between devices  321 us (33%)
  local copies, waits for them, and re-layouts  127 us (13%)
  other arithmetic  76.5 us (8%)
  blocking collectives  17.5 us (2%)
  between operations  13.7 us (1%)
    all_gather x1, waiting for transfers between devices, on_device(): extended = lax.all_gather(paired, 'tok', axis=1, tiled=True)  321 us
    dot_general x18, matrix products, attend(): jnp.einsum('tqd,tkd->tqk', query_block[:, :, lower:upper], key_window[:,...  235 us
    dot_general x18, matrix products, attend(): jnp.einsum('tqk,tkd->tqd', weights.astype(jnp.bfloat16), value_window[:,...  173 us
    reduce_sum x3, other arithmetic, attend(): weight_sum = jnp.sum(weights, axis=2, keepdims=True)  63.2 us
    gather x3, local copies, waits for them, and re-layouts, attend(): value_tiles[tile_ids].reshape(2, WINDOW_SLOTS * TILE_TOKENS, local_width)  47.6 us
    gather x3, local copies, waits for them, and re-layouts, attend(): key_tiles[tile_ids].reshape(2, WINDOW_SLOTS * TILE_TOKENS, local_width)  46.7 us
    slice x1, local copies, waits for them, and re-layouts, on_device(): value_tiles = extended[1].reshape(-1, TILE_TOKENS, local_width)  26.5 us
  transfers between devices with their start and end apart: 1, of which 1 were waited for; matrix products, arithmetic and copies ran while one was open for 0% of the time, Pallas kernels for 0%

commit v1 on v0

--- a/solution.py
+++ b/solution.py
@@ -8,6 +8,12 @@
 MODEL_DIM = 3072
 TILE_TOKENS = 256
 WINDOW_SLOTS = 27
+
+
+def lift_shelves(sample, d0):
+    side_arr = list(sample.shape[1:])
+    side_arr[d0] *= sample.shape[0]
+    return jnp.moveaxis(sample, 0, d0).reshape(side_arr)
 
 
 def square_sums(source):
@@ -30,7 +36,21 @@
     query_normed = normalize_rows(query_states, query_total, query_gain)
     sent_keys = normalize_rows(key_states, key_total, key_gain)
     paired = jnp.stack([sent_keys, value_states])
-    extended = lax.all_gather(paired, "tok", axis=1, tiled=True)
+    total_devices = lax.axis_size("tok")
+    pile = tuple(((u, (u + 1) % total_devices) for u in range(total_devices)))
+    entries = tuple(((h, no) for no, h in pile))
+    passed, back = ([], [])
+    for src_i in tuple(range(total_devices - 1)):
+        if src_i % 2 == 0:
+            y_new = lax.ppermute(passed[-1] if passed else paired, axis_name="tok", perm=pile)
+            passed.append(y_new)
+        else:
+            back.append(lax.ppermute(back[-1] if back else paired, axis_name="tok", perm=entries))
+    r1 = jnp.stack([*passed[::-1], paired, *back], 0)
+    carry = lax.axis_index("tok")
+    b_now = carry - len(passed)
+    r1 = r1[(jnp.arange(total_devices) - b_now) % total_devices]
+    extended = lift_shelves(r1, 1)
     key_window_rows = extended[0]
     heads_here = local_width // HEAD_DIM
     key_tiles = key_window_rows.reshape(-1, TILE_TOKENS, local_width)

time: 971 us -> 1130 us (1.16)
  local copies, waits for them, and re-layouts: 127 us -> 216 us
  waiting for transfers between devices: 321 us -> 357 us
  other arithmetic: 76.5 us -> 104 us
  between operations: 13.7 us -> 1.2 us
    ppermute x0 -> x7, waiting for transfers between devices: none -> 357 us  [the longest x4 357 us: on_device(): lax.ppermute(passed[-1] if passed else paired, axis_name='tok', perm=pile)]
    all_gather x1 -> x0, waiting for transfers between devices: 321 us -> none  [on_device(): extended = lax.all_gather(paired, 'tok', axis=1, tiled=True)]
    gather x0 -> x4, local copies, waits for them, and re-layouts: none -> 58.4 us  [on_device(): r1 = r1[(jnp.arange(total_devices) - b_now) % total_devices]]
    unnamed x6 -> x24, local copies, waits for them, and re-layouts: 0.01 us -> 28.6 us
    transpose x0 -> x1, other arithmetic: none -> 25.9 us  [lift_shelves(): return jnp.moveaxis(sample, 0, d0).reshape(side_arr)]
  transfers between devices with their start and end apart: 1 -> 7, of which waited for: 1 -> 4; matrix products, arithmetic and copies ran while one was open for 0% -> 3% of each run, Pallas kernels for 0% -> 0%
where the time goes in v1:
time: 1130 us; the launch traced here: 1120 us
  matrix products  408 us (36%)
  waiting for transfers between devices  357 us (32%)
  local copies, waits for them, and re-layouts  216 us (19%)
  other arithmetic  104 us (9%)
  blocking collectives  17.5 us (2%)
    ppermute x4, waiting for transfers between devices, on_device(): lax.ppermute(passed[-1] if passed else paired, axis_name='tok', perm=pile)  357 us
    dot_general x18, matrix products, attend(): jnp.einsum('tqd,tkd->tqk', query_block[:, :, lower:upper], key_window[:,...  235 us
    dot_general x18, matrix products, attend(): jnp.einsum('tqk,tkd->tqd', weights.astype(jnp.bfloat16), value_window[:,...  173 us
    reduce_sum x3, other arithmetic, attend(): weight_sum = jnp.sum(weights, axis=2, keepdims=True)  63.2 us
    gather x4, local copies, waits for them, and re-layouts, on_device(): r1 = r1[(jnp.arange(total_devices) - b_now) % total_devices]  58.4 us
    gather x3, local copies, waits for them, and re-layouts, attend(): value_tiles[tile_ids].reshape(2, WINDOW_SLOTS * TILE_TOKENS, local_width)  47.5 us
    gather x3, local copies, waits for them, and re-layouts, attend(): key_tiles[tile_ids].reshape(2, WINDOW_SLOTS * TILE_TOKENS, local_width)  46.7 us
    unnamed x24, local copies, waits for them, and re-layouts  28.6 us
  transfers between devices with their start and end apart: 7, of which 4 were waited for; matrix products, arithmetic and copies ran while one was open for 3% of the time, Pallas kernels for 0%

profile of v1, /device:TPU:0, one launch (start us, length us, event | category | flops | bytes accessed | tf_op | source)
XLA Modules:
  0.0 1118.8 jit_solution(6799116763743841667)
XLA Ops:
  4.4 17.5 %all-reduce = (f32[1536]{0:T(1024)S(1)}, f32[1536]{0:T(1024)S(1)}) all-reduce(f32[1536]{0:T(1024)S(1)} %fusion.168, f32[1536]{0:T(1024)S(1)} %fusion.171), channel_id=1, replica_groups=mesh['tok'=8,'head'=4] {'head'}, use_global_device_ids=true, to_apply=%region_1.0 | all-reduce | flops 3072 | bytes 24576 | tf_op jit(solution)/shard_map/psum | solution.py:35
  26.4 55.3 %collective-permute-done = bf16[2,1536,768]{2,1,0:T(8,128)(2,1)S(1)} collective-permute-done((bf16[2,1536,768]{2,1,0:T(8,128)(2,1)S(1)}, bf16[2,1536,768]{2,1,0:T(8,128)(2,1)S(1)}, u32[]{:S(2)}, u32[]{:S(2)}) %collective-permute-start) | collective-permute-done | bytes 4718624 | tf_op jit(solution)/shard_map/ppermute | solution.py:45
  87.4 102.1 %collective-permute-done.1 = bf16[2,1536,768]{2,1,0:T(8,128)(2,1)S(1)} collective-permute-done((bf16[2,1536,768]{2,1,0:T(8,128)(2,1)S(1)}, bf16[2,1536,768]{2,1,0:T(8,128)(2,1)S(1)}, u32[]{:S(2)}, u32[]{:S(2)}) %collective-permute-start.1) | collective-permute-done | bytes 4718624 | tf_op jit(solution)/shard_map/ppermute | solution.py:45
  191.6 3.5 collective-permute-start.5
  195.2 101.5 %collective-permute-done.2 = bf16[2,1536,768]{2,1,0:T(8,128)(2,1)} collective-permute-done((bf16[2,1536,768]{2,1,0:T(8,128)(2,1)S(1)}, bf16[2,1536,768]{2,1,0:T(8,128)(2,1)}, u32[]{:S(2)}, u32[]{:S(2)}) %collective-permute-start.2) | collective-permute-done | bytes 4718624 | tf_op jit(solution)/shard_map/ppermute | solution.py:45
  296.8 3.8 fusion.170
  300.6 3.6 collective-permute-start.6
  304.2 98.5 %collective-permute-done.3 = bf16[2,1536,768]{2,1,0:T(8,128)(2,1)} collective-permute-done((bf16[2,1536,768]{2,1,0:T(8,128)(2,1)}, bf16[2,1536,768]{2,1,0:T(8,128)(2,1)}, u32[]{:S(2)}, u32[]{:S(2)}) %collective-permute-start.3) | collective-permute-done | bytes 4718624 | tf_op jit(solution)/shard_map/ppermute | solution.py:45
  402.7 4.8 bitcast_dynamic-update-slice_fusion.7
  407.5 5.0 bitcast_dynamic-update-slice_fusion.6
  419.9 4.9 bitcast_dynamic-update-slice_fusion.2
  424.8 4.7 bitcast_dynamic-update-slice_fusion.1
  432.0 25.4 %fusion.178 = (bf16[8,2,512,768]{3,2,1,0:T(8,128)(2,1)}, bf16[8,2,512,768]{3,2,1,0:T(8,128)(2,1)}, bf16[8,2,512,768]{3,2,1,0:T(8,128)(2,1)}) fusion(bf16[8,2,1536,768]{3,2,1,0:T(8,128)(2,1)} %bitcast_dynamic-update-slice_fusion), kind=kLoop, calls=%fused_computation.146 | loop fusion | bytes 75497472 | tf_op jit(solution)/shard_map/gather | solution.py:52
  457.4 11.0 gather_fusion.2
  468.4 11.0 gather_fusion.3
  479.5 10.9 gather_fusion.4
  490.4 25.9 %maximum_bitcast_fusion = bf16[2,8,1536,768]{3,2,0,1:T(8,128)(2,1)} fusion(bf16[8,2,512,768]{3,2,1,0:T(8,128)(2,1)} %gather_fusion.4, bf16[8,2,512,768]{3,2,1,0:T(8,128)(2,1)} %gather_fusion.3, bf16[8,2,512,768]{3,2,1,0:T(8,128)(2,1)} %gather_fusion.2), kind=kLoop, calls=%fused_computation.113 | loop fusion | flops 113246208 | bytes 75497472 | tf_op jit(solution)/shard_map/transpose | solution.py:16
  516.4 25.8 %fusion.177 = (bf16[1,8,1536,768]{3,2,0,1:T(8,128)(2,1)}, bf16[1,8,1536,768]{3,2,0,1:T(8,128)(2,1)}) fusion(bf16[2,8,1536,768]{3,2,0,1:T(8,128)(2,1)} %maximum_bitcast_fusion), kind=kLoop, calls=%fused_computation.145 | loop fusion | bytes 75497472 | tf_op jit(solution)/shard_map/slice | solution.py:57
  542.1 575.5 %while.10 = (s32[]{:T(128)}, bf16[3,2,256,768]{3,2,1,0:T(8,128)(2,1)}, s32[3]{0:T(128)S(1)}, pred[6,27]{1,0:T(8,128)(4,1)S(1)}, bf16[6,256,768]{2,1,0:T(8,128)(2...) while((s32[]{:T(128)}, ...), condition=%wide.region_17.18_spmd, body=%wide.region_4.17_spmd.sunk | while | flops 11105987584 | bytes 443850720 | solution.py:98
  544.0 15.5 %gather_fusion.1 = bf16[54,256,768]{2,1,0:T(8,128)(2,1)} fusion(bf16[48,256,768]{2,1,0:T(8,128)(2,1)} %get-tuple-element.204, s32[1024]{0:T(1024)S(1)} %pad_clamp_fusion.3), kind=kCustom, calls=%fused_computation.clone.1 | custom fusion | bytes 42467544 | tf_op jit(solution)/shard_map/while/body/eval_jaxpr/gather | solution.py:69
  559.5 9.0 fusion.232
  568.7 10.7 fusion.233
  579.4 9.2 fusion.234
  588.6 9.0 fusion.235
  597.6 9.1 fusion.236
  606.8 31.3 %fusion.237 = (f32[2,256]{1,0:T(2,128)S(1)}, f32[2,256]{1,0:T(2,128)S(1)}, f32[2,256]{1,0:T(2,128)S(1)}, f32[2,256]{1,0:T(2,128)S(1)}, f32[2,256]{1,0:T(2,128)S(...) fusion(f32[2,256,6912]{2,1,0:T(8,128)} %get-tuple-element.151, f32[2,256]{1,0:T(2,128)S(1)} %get-tuple-element.152, ...), kind=kOutput, calls=%fused_computation.33.clone.1 | convolution fusion | flops 976745472 | bytes 88634888 | tf_op jit(solution)/shard_map/while/body/eval_jaxpr/tqd,tkd->tqk/dot_general | solution.py:77
  638.1 21.1 %fusion.239 = (f32[2,256]{1,0:T(2,128)S(1)}, f32[2,256]{1,0:T(2,128)S(1)}, f32[2,256]{1,0:T(2,128)S(1)}, f32[2,256]{1,0:T(2,128)S(1)}) fusion(f32[2,256,6912]{2,1,0:T(8,128)} %fusion.236, f32[2,256]{1,0:T(2,128)S(1)} %get-tuple-element.156, pred[2,6912]{1,0:T(4,128)(4,1)S(1)} %bitcast.63, f32[2,256]{1,0:T(2,128)S(1)} %get-tuple-element.155, ...), kind=kLoop, calls=%fused_computation.31.clone.1 | loop fusion | flops 56621056 | bytes 56653312 | tf_op jit(solution)/shard_map/while/body/eval_jaxpr/reduce_sum | solution.py:88
  659.2 15.6 %gather_fusion = bf16[54,256,768]{2,1,0:T(8,128)(2,1)} fusion(bf16[48,256,768]{2,1,0:T(8,128)(2,1)} %get-tuple-element.205, s32[1024]{0:T(1024)S(1)} %pad_clamp_fusion.3), kind=kCustom, calls=%fused_computation.1.clone.1 | custom fusion | bytes 42467544 | tf_op jit(solution)/shard_map/while/body/eval_jaxpr/gather | solution.py:70
  674.8 9.5 fusion.238
  684.4 9.5 fusion.240
  693.9 9.6 fusion.241
  703.5 9.8 fusion.242
  713.2 9.6 fusion.243
  722.8 9.6 fusion.244
  735.5 15.6 %gather_fusion.1 = bf16[54,256,768]{2,1,0:T(8,128)(2,1)} fusion(bf16[48,256,768]{2,1,0:T(8,128)(2,1)} %get-tuple-element.204, s32[1024]{0:T(1024)S(1)} %pad_clamp_fusion.3), kind=kCustom, calls=%fused_computation.clone.1 | custom fusion | bytes 42467544 | tf_op jit(solution)/shard_map/while/body/eval_jaxpr/gather | solution.py:69
  751.1 9.0 fusion.232
  760.3 10.7 fusion.233
  771.0 9.2 fusion.234
  780.2 9.0 fusion.235
  789.2 9.1 fusion.236
  798.3 31.1 %fusion.237 = (f32[2,256]{1,0:T(2,128)S(1)}, f32[2,256]{1,0:T(2,128)S(1)}, f32[2,256]{1,0:T(2,128)S(1)}, f32[2,256]{1,0:T(2,128)S(1)}, f32[2,256]{1,0:T(2,128)S(...) fusion(f32[2,256,6912]{2,1,0:T(8,128)} %get-tuple-element.151, f32[2,256]{1,0:T(2,128)S(1)} %get-tuple-element.152, ...), kind=kOutput, calls=%fused_computation.33.clone.1 | convolution fusion | flops 976745472 | bytes 88634888 | tf_op jit(solution)/shard_map/while/body/eval_jaxpr/tqd,tkd->tqk/dot_general | solution.py:77
  829.4 21.1 %fusion.239 = (f32[2,256]{1,0:T(2,128)S(1)}, f32[2,256]{1,0:T(2,128)S(1)}, f32[2,256]{1,0:T(2,128)S(1)}, f32[2,256]{1,0:T(2,128)S(1)}) fusion(f32[2,256,6912]{2,1,0:T(8,128)} %fusion.236, f32[2,256]{1,0:T(2,128)S(1)} %get-tuple-element.156, pred[2,6912]{1,0:T(4,128)(4,1)S(1)} %bitcast.63, f32[2,256]{1,0:T(2,128)S(1)} %get-tuple-element.155, ...), kind=kLoop, calls=%fused_computation.31.clone.1 | loop fusion | flops 56621056 | bytes 56653312 | tf_op jit(solution)/shard_map/while/body/eval_jaxpr/reduce_sum | solution.py:88
  850.5 15.8 %gather_fusion = bf16[54,256,768]{2,1,0:T(8,128)(2,1)} fusion(bf16[48,256,768]{2,1,0:T(8,128)(2,1)} %get-tuple-element.205, s32[1024]{0:T(1024)S(1)} %pad_clamp_fusion.3), kind=kCustom, calls=%fused_computation.1.clone.1 | custom fusion | bytes 42467544 | tf_op jit(solution)/shard_map/while/body/eval_jaxpr/gather | solution.py:70
  866.4 9.6 fusion.238
  875.9 9.6 fusion.240
  885.5 9.6 fusion.241
  895.0 9.9 fusion.242
  905.0 9.6 fusion.243
  914.6 9.6 fusion.244
  927.0 15.6 %gather_fusion.1 = bf16[54,256,768]{2,1,0:T(8,128)(2,1)} fusion(bf16[48,256,768]{2,1,0:T(8,128)(2,1)} %get-tuple-element.204, s32[1024]{0:T(1024)S(1)} %pad_clamp_fusion.3), kind=kCustom, calls=%fused_computation.clone.1 | custom fusion | bytes 42467544 | tf_op jit(solution)/shard_map/while/body/eval_jaxpr/gather | solution.py:69
  942.6 9.1 fusion.232
  951.8 10.7 fusion.233
  962.5 9.2 fusion.234
  971.7 9.0 fusion.235
  980.7 9.1 fusion.236
  989.9 31.1 %fusion.237 = (f32[2,256]{1,0:T(2,128)S(1)}, f32[2,256]{1,0:T(2,128)S(1)}, f32[2,256]{1,0:T(2,128)S(1)}, f32[2,256]{1,0:T(2,128)S(1)}, f32[2,256]{1,0:T(2,128)S(...) fusion(f32[2,256,6912]{2,1,0:T(8,128)} %get-tuple-element.151, f32[2,256]{1,0:T(2,128)S(1)} %get-tuple-element.152, ...), kind=kOutput, calls=%fused_computation.33.clone.1 | convolution fusion | flops 976745472 | bytes 88634888 | tf_op jit(solution)/shard_map/while/body/eval_jaxpr/tqd,tkd->tqk/dot_general | solution.py:77
  1021.0 21.1 %fusion.239 = (f32[2,256]{1,0:T(2,128)S(1)}, f32[2,256]{1,0:T(2,128)S(1)}, f32[2,256]{1,0:T(2,128)S(1)}, f32[2,256]{1,0:T(2,128)S(1)}) fusion(f32[2,256,6912]{2,1,0:T(8,128)} %fusion.236, f32[2,256]{1,0:T(2,128)S(1)} %get-tuple-element.156, pred[2,6912]{1,0:T(4,128)(4,1)S(1)} %bitcast.63, f32[2,256]{1,0:T(2,128)S(1)} %get-tuple-element.155, ...), kind=kLoop, calls=%fused_computation.31.clone.1 | loop fusion | flops 56621056 | bytes 56653312 | tf_op jit(solution)/shard_map/while/body/eval_jaxpr/reduce_sum | solution.py:88
  1042.1 16.0 %gather_fusion = bf16[54,256,768]{2,1,0:T(8,128)(2,1)} fusion(bf16[48,256,768]{2,1,0:T(8,128)(2,1)} %get-tuple-element.205, s32[1024]{0:T(1024)S(1)} %pad_clamp_fusion.3), kind=kCustom, calls=%fused_computation.1.clone.1 | custom fusion | bytes 42467544 | tf_op jit(solution)/shard_map/while/body/eval_jaxpr/gather | solution.py:70
  1058.1 9.5 fusion.238
  1067.6 9.5 fusion.240
  1077.2 9.6 fusion.241
  1086.8 9.7 fusion.242
  1096.5 9.6 fusion.243
  1106.0 9.6 fusion.244
  (70 shorter events, 32.8 us)
Async XLA Ops:
  0.0 296.7 %copy-start.3 = (s32[6,27]{1,0:T(8,128)S(1)}, s32[6,27]{1,0:T(8,128)}, u32[]{:S(2)}) copy-start(s32[6,27]{1,0:T(8,128)} %param.13) | copy-start | bytes 1948
  0.0 296.8 %copy-start.4 = (f32[768]{0:T(1024)S(1)}, f32[768]{0:T(1024)}, u32[]{:S(2)}) copy-start(f32[768]{0:T(1024)} %param.11) | copy-start | bytes 9220
  26.3 55.4 %collective-permute-start = (bf16[2,1536,768]{2,1,0:T(8,128)(2,1)S(1)}, bf16[2,1536,768]{2,1,0:T(8,128)(2,1)S(1)}, u32[]{:S(2)}, u32[]{:S(2)}) collective-permute-start(bf16[2,1536,768]{2,1,0:T(8,128)(2,1)S(1)} %pad_maximum_fusion), channel_id=1, source_target_pairs={{0,4},{4,8},{8,12},{12,16},{16,20},{20,24},{24,28},{28,0},{1,5},{5... | collective-permute-start | bytes 14155784 | tf_op jit(solution)/shard_map/ppermute | solution.py:45
  81.7 2.2 copy-start.1
  83.9 105.6 %collective-permute-start.1 = (bf16[2,1536,768]{2,1,0:T(8,128)(2,1)S(1)}, bf16[2,1536,768]{2,1,0:T(8,128)(2,1)S(1)}, u32[]{:S(2)}, u32[]{:S(2)}) collective-permute-start(bf16[2,1536,768]{2,1,0:T(8,128)(2,1)S(1)} %collective-permute-done), channel_id=1, source_target_pairs={{0,4},{4,8},{8,12},{12,16},{16,20},{20,24},{24,28},{28,0},{1,5},{5... | collective-permute-start | bytes 14155784 | tf_op jit(solution)/shard_map/ppermute | solution.py:45
  83.9 107.7 %collective-permute-start.4 = (bf16[2,1536,768]{2,1,0:T(8,128)(2,1)S(1)}, bf16[2,1536,768]{2,1,0:T(8,128)(2,1)}, u32[]{:S(2)}, u32[]{:S(2)}) collective-permute-start(bf16[2,1536,768]{2,1,0:T(8,128)(2,1)S(1)} %pad_maximum_fusion), channel_id=1, source_target_pairs={{4,0},{8,4},{12,8},{16,12},{20,16},{24,20},{28,24},{0,28},{5,1},{9... | collective-permute-start | bytes 14155784 | tf_op jit(solution)/shard_map/ppermute | solution.py:48
  189.5 2.1 copy-start.2
  191.6 105.1 %collective-permute-start.2 = (bf16[2,1536,768]{2,1,0:T(8,128)(2,1)S(1)}, bf16[2,1536,768]{2,1,0:T(8,128)(2,1)}, u32[]{:S(2)}, u32[]{:S(2)}) collective-permute-start(bf16[2,1536,768]{2,1,0:T(8,128)(2,1)S(1)} %collective-permute-done.1), channel_id=1, source_target_pairs={{0,4},{4,8},{8,12},{12,16},{16,20},{20,24},{24,28},{28,0},{1,5},{5... | collective-permute-start | bytes 14155784 | tf_op jit(solution)/shard_map/ppermute | solution.py:45
  191.6 109.0 %collective-permute-start.5 = (bf16[2,1536,768]{2,1,0:T(8,128)(2,1)}, bf16[2,1536,768]{2,1,0:T(8,128)(2,1)}, u32[]{:S(2)}, u32[]{:S(2)}) collective-permute-start(bf16[2,1536,768]{2,1,0:T(8,128)(2,1)} %collective-permute-done.4), channel_id=1, source_target_pairs={{4,0},{8,4},{12,8},{16,12},{20,16},{24,20},{28,24},{0,28},{5,1},{9... | collective-permute-start | bytes 14155784 | tf_op jit(solution)/shard_map/ppermute | solution.py:48
  296.7 106.0 %collective-permute-start.3 = (bf16[2,1536,768]{2,1,0:T(8,128)(2,1)}, bf16[2,1536,768]{2,1,0:T(8,128)(2,1)}, u32[]{:S(2)}, u32[]{:S(2)}) collective-permute-start(bf16[2,1536,768]{2,1,0:T(8,128)(2,1)} %collective-permute-done.2), channel_id=1, source_target_pairs={{0,4},{4,8},{8,12},{12,16},{16,20},{20,24},{24,28},{28,0},{1,5},{5... | collective-permute-start | bytes 14155784 | tf_op jit(solution)/shard_map/ppermute | solution.py:45
  296.7 115.9 %slice-start.2 = ((s8[4718592]{0:T(1024)(128)(4,1)}), s8[4194304]{0:T(1024)(128)(4,1)S(1)}, s32[]{:S(2)}) async-start(s8[4718592]{0:T(1024)(128)(4,1)} %bitcast.74), calls=%async_computation.2 | async-start | bytes 8388608
  300.6 112.0 %slice-start.3 = ((s8[4718592]{0:T(1024)(128)(4,1)}), s8[524288]{0:T(1024)(128)(4,1)S(1)}, s32[]{:S(2)}) async-start(s8[4718592]{0:T(1024)(128)(4,1)} %bitcast.74), calls=%async_computation.3 | async-start | bytes 1048576
  300.6 114.4 %slice-start = ((s8[4718592]{0:T(1024)(128)(4,1)}), s8[4194304]{0:T(1024)(128)(4,1)S(1)}, s32[]{:S(2)}) async-start(s8[4718592]{0:T(1024)(128)(4,1)} %bitcast.72), calls=%async_computation | async-start | bytes 8388608
  300.6 128.9 %collective-permute-start.6 = (bf16[2,1536,768]{2,1,0:T(8,128)(2,1)}, bf16[2,1536,768]{2,1,0:T(8,128)(2,1)S(1)}, u32[]{:S(2)}, u32[]{:S(2)}) collective-permute-start(bf16[2,1536,768]{2,1,0:T(8,128)(2,1)} %collective-permute-done.5), channel_id=1, source_target_pairs={{4,0},{8,4},{12,8},{16,12},{20,16},{24,20},{28,24},{0,28},{5,1},{9... | collective-permute-start | bytes 14155784 | tf_op jit(solution)/shard_map/ppermute | solution.py:48
  407.5 7.5 slice-start.1
  407.5 9.9 copy-start
